TPU v7x, 512 devices: a whole 4x4x16 slice. The times are simulated.
512 devices in a mesh: seq: 64 (over x, z), tp: 8 (over y, core).
Axes of the slice: x: 4, y: 4, z: 16, core: 2. Of those that a mesh axis runs over, the one named last changes fastest.
Arguments:
- queries: bfloat16 [64, 4, 8192], P('seq', None, 'tp'), may hold values from -40 to 40
- new_keys: bfloat16 [64, 4, 1024], P('seq', None, 'tp'), may hold values from -6 to 6
- new_values: bfloat16 [64, 4, 1024], P('seq', None, 'tp'), may hold values from -6 to 6
- prefix_keys: bfloat16 [8, 12288, 1024], P(None, 'seq', 'tp'), may hold values from -8 to 8
- prefix_values: bfloat16 [8, 12288, 1024], P(None, 'seq', 'tp'), may hold values from -6 to 6
- page_keys: bfloat16 [1024, 64, 1024], P('seq', None, 'tp'), may hold values from -6 to 6
- page_values: bfloat16 [1024, 64, 1024], P('seq', None, 'tp'), may hold values from -6 to 6
- out_weight: bfloat16 [8192, 8192], P('tp', 'seq'), may hold values from -0.5 to 0.5
- group_of: int32 [64], replicated, may hold values from 0 to 7, as said below
- prefix_len: int32 [8], replicated, may hold values from 2 to 12288, as said below
- total_len: int32 [64], replicated, may hold values from 3 to 16384, as said below
- page_owner: int32 [1024], P('seq'), may hold values from 0 to 63, as said below
- page_slot: int32 [1024], P('seq'), may hold values from 0 to 63, as said below
- new_valid: int32 [64, 4], replicated, may hold values from 0 to 1, as said below
Outputs:
- attn_out: bfloat16 [256, 8192], P('tp', 'seq')
Inputs may be any that keep to these rules, and one draw needn't show every extreme that they name: `group_of`: every one of the 8 groups has at least one request. `prefix_len`: some group's prefix holds exactly 12288 tokens. `page_owner`: every request owns at least one page and at most 64 pages; one request owns exactly 64. `page_slot`: the pages of one request carry the slots 0, 1, 2 and so on, each once. A request's pages are full except the one of its highest slot, which holds 1 to 64 tokens; total_len is its group's prefix length plus these tokens. `new_valid`: each row is a run of ones followed by zeros, and its first entry is one.
All inputs are finite; a program needn't handle non-finite values.
Results may differ from a plain program's by a relative error of at most 0.022.
Values may be sent and summed in bfloat16 or wider, within the bound.
No kernel may reach another device: no remote copies, remote signals or barrier semaphores. Data moves between devices by JAX's collectives and lax.ppermute only.
A program may use at most 192 MiB of HBM per device.

v0:
```python
import jax
import jax.numpy as jnp
from jax import lax
from jax.sharding import PartitionSpec as P

HEAD_DIM = 128
HPK = 8
GROUPS = 8
NEW = 4
NEG = -1e30


def merged(part, axis, combine):
    gathered = jax.tree.map(lambda a: lax.all_gather(a, axis), part)

    def take(source):
        return jax.tree.map(lambda a: lax.dynamic_index_in_dim(a, source, 0, False), gathered)

    return lax.fori_loop(
        1, lax.axis_size(axis), lambda source, state: combine(state, take(source)), take(0)
    )


def softmax_part(scores, key_mask):
    masked = jnp.where(key_mask, scores, NEG)
    row_peak = jnp.max(masked, axis=-1)
    weights = jnp.where(key_mask, jnp.exp(masked - row_peak[..., None]), 0.0)
    return (row_peak, jnp.sum(weights, axis=-1), weights.astype(jnp.bfloat16))


def combine(first_part, second_part):
    peak_a, total_a, out_a = first_part
    peak_b, total_b, out_b = second_part
    top_peak = jnp.maximum(peak_a, peak_b)
    factor_a = jnp.exp(peak_a - top_peak)
    factor_b = jnp.exp(peak_b - top_peak)
    return (
        top_peak,
        total_a * factor_a + total_b * factor_b,
        out_a * factor_a[..., None] + out_b * factor_b[..., None],
    )


def local(
    queries,
    new_keys,
    new_values,
    prefix_keys,
    prefix_values,
    page_keys,
    page_values,
    out_weight,
    group_of,
    prefix_len,
    total_len,
    page_owner,
    page_slot,
    new_valid,
):
    req_dev = queries.shape[0]
    seq_count = lax.axis_size("seq")
    requests = req_dev * seq_count
    kv_local = new_keys.shape[2] // HEAD_DIM
    heads_local = kv_local * HPK
    score_scale = HEAD_DIM ** (-0.5)
    seq_idx = lax.axis_index("seq")
    gathered = lax.all_gather(queries, "seq", axis=0, tiled=True)
    query_all = gathered.reshape(requests, NEW, kv_local, HPK, HEAD_DIM)
    group_hot = group_of[:, None] == jnp.arange(GROUPS, dtype=jnp.int32)[None, :]
    own_prefix = jnp.sum(jnp.where(group_hot, prefix_len[None, :], 0), axis=1)
    suffix_len = total_len - own_prefix
    pre_dev = prefix_keys.shape[1]
    positions = seq_idx * pre_dev + jnp.arange(pre_dev, dtype=jnp.int32)
    pre_keys = prefix_keys.reshape(GROUPS, pre_dev, kv_local, HEAD_DIM)
    pre_values = prefix_values.reshape(GROUPS, pre_dev, kv_local, HEAD_DIM)
    partial_value = (
        jnp.full((requests, NEW, kv_local, HPK), NEG, jnp.float32),
        jnp.zeros((requests, NEW, kv_local, HPK), jnp.float32),
        jnp.zeros((requests, NEW, kv_local, HPK, HEAD_DIM), jnp.float32),
    )
    for group_idx in range(GROUPS):
        scores = (
            jnp.einsum(
                "rjkhd,ikd->rjkhi",
                query_all,
                pre_keys[group_idx],
                preferred_element_type=jnp.float32,
            )
            * score_scale
        )
        member = group_hot[:, group_idx]
        live_keys = positions < prefix_len[group_idx]
        key_mask = member[:, None, None, None, None] & live_keys[None, None, None, None, :]
        row_peak, row_total, weights = softmax_part(scores, key_mask)
        values = jnp.einsum(
            "rjkhi,ikd->rjkhd", weights, pre_values[group_idx], preferred_element_type=jnp.float32
        )
        chosen = member[:, None, None, None]
        partial_value = (
            jnp.where(chosen, row_peak, partial_value[0]),
            jnp.where(chosen, row_total, partial_value[1]),
            jnp.where(chosen[..., None], values, partial_value[2]),
        )
    prefix_part = partial_value
    page_count = page_keys.shape[0]
    page_len = page_keys.shape[1]
    key_pages = page_keys.reshape(page_count, page_len, kv_local, HEAD_DIM)
    value_pages = page_values.reshape(page_count, page_len, kv_local, HEAD_DIM)
    owner_hot = page_owner[:, None] == jnp.arange(requests, dtype=jnp.int32)[None, :]
    own_suffix = jnp.sum(jnp.where(owner_hot, suffix_len[None, :], 0), axis=1)
    page_queries = jnp.take(query_all, page_owner, axis=0)
    scores = (
        jnp.einsum("pjkhd,pikd->pjkhi", page_queries, key_pages, preferred_element_type=jnp.float32)
        * score_scale
    )
    offsets = page_slot[:, None] * page_len + jnp.arange(page_len, dtype=jnp.int32)[None, :]
    live_keys = offsets < own_suffix[:, None]
    page_peak, page_total, weights = softmax_part(scores, live_keys[:, None, None, None, :])
    page_out = jnp.einsum(
        "pjkhi,pikd->pjkhd", weights, value_pages, preferred_element_type=jnp.float32
    )
    owner_wide = owner_hot[:, :, None, None, None]
    device_peak = jnp.max(jnp.where(owner_wide, page_peak[:, None], NEG), axis=0)
    page_back = jnp.max(jnp.where(owner_wide, device_peak[None], NEG), axis=1)
    factor = jnp.exp(page_peak - page_back)
    owner_float = owner_hot.astype(jnp.float32)
    suffix_total = jnp.einsum(
        "pr,pjkh->rjkh", owner_float, page_total * factor, precision=lax.Precision.HIGHEST
    )
    suffix_out = jnp.einsum(
        "pr,pjkhd->rjkhd",
        owner_float,
        page_out * factor[..., None],
        precision=lax.Precision.HIGHEST,
    )
    partial_value = combine(prefix_part, (device_peak, suffix_total, suffix_out))
    row_start = seq_idx * req_dev
    local_queries = queries.reshape(req_dev, NEW, kv_local, HPK, HEAD_DIM)
    local_keys = new_keys.reshape(req_dev, NEW, kv_local, HEAD_DIM)
    local_values = new_values.reshape(req_dev, NEW, kv_local, HEAD_DIM)
    valid_local = lax.dynamic_slice_in_dim(new_valid, row_start, req_dev, 0)
    scores = (
        jnp.einsum(
            "rjkhd,rikd->rjkhi", local_queries, local_keys, preferred_element_type=jnp.float32
        )
        * score_scale
    )
    causal = jnp.arange(NEW, dtype=jnp.int32)[None, :] <= jnp.arange(NEW, dtype=jnp.int32)[:, None]
    key_mask = causal[None, :, None, None, :] & (valid_local[:, None, None, None, :] == 1)
    row_peak, row_total, weights = softmax_part(scores, key_mask)
    new_out = jnp.einsum(
        "rjkhi,rikd->rjkhd", weights, local_values, preferred_element_type=jnp.float32
    )
    own_rows = (
        lax.dynamic_slice_in_dim(partial_value[0], row_start, req_dev, 0),
        lax.dynamic_slice_in_dim(partial_value[1], row_start, req_dev, 0),
        lax.dynamic_slice_in_dim(partial_value[2], row_start, req_dev, 0),
    )
    own_part = combine(own_rows, (row_peak, row_total, new_out))
    partial_value = (
        lax.dynamic_update_slice_in_dim(partial_value[0], own_part[0], row_start, 0),
        lax.dynamic_update_slice_in_dim(partial_value[1], own_part[1], row_start, 0),
        lax.dynamic_update_slice_in_dim(partial_value[2], own_part[2], row_start, 0),
    )
    final_peak, final_total, final_out = merged(partial_value, "seq", combine)
    valid_rows = new_valid.astype(jnp.float32)[:, :, None, None, None]
    attention = (final_out / final_total[..., None] * valid_rows).astype(jnp.bfloat16)
    attention = attention.reshape(requests * NEW, heads_local * HEAD_DIM)
    terms = jnp.dot(attention, out_weight, preferred_element_type=jnp.float32)
    summed = lax.psum_scatter(terms.astype(jnp.bfloat16), "tp", scatter_dimension=0, tiled=True)
    return summed


def solution(mesh):
    placed = (
        P("seq", None, "tp"),
        P("seq", None, "tp"),
        P("seq", None, "tp"),
        P(None, "seq", "tp"),
        P(None, "seq", "tp"),
        P("seq", None, "tp"),
        P("seq", None, "tp"),
        P("tp", "seq"),
        P(),
        P(),
        P(),
        P("seq"),
        P("seq"),
        P(),
    )
    return jax.shard_map(
        local, mesh=mesh, in_specs=placed, out_specs=P("tp", "seq"), check_vma=False
    )
```

profile of v0, /device:TPU:2, one launch (start us, length us, event | category | flops | bytes accessed | tf_op | source)
XLA Modules:
  0.0 936.6 jit_solution(16358263161853906716)
XLA Ops:
  12.8 106.3 %all_gather.25 = bf16[64,4,1024]{2,1,0:T(4,128)(2,1)S(1)} all-gather(bf16[1,4,1024]{2,1,0:T(4,128)(2,1)} %param.16), channel_id=1, replica_groups=mesh['seq'=64,'tp'=8] {'seq'}, dimensions={0}, use_global_device_ids=true | all-gather | bytes 532480 | tf_op jit(solution)/shard_map/all_gather | solution.py:67
  126.1 1.9 fusion.11
  129.3 1.9 fusion.10
  131.3 2.0 fusion.9
  149.6 2.3 fusion.58
  151.9 2.4 fusion.57
  154.3 2.3 fusion.56
  156.6 2.3 fusion.55
  159.0 2.3 fusion.54
  161.3 2.3 fusion.53
  163.6 2.3 fusion.52
  169.9 2.4 fusion.72
  185.5 3.2 fusion.150
  191.4 102.1 %all_gather.27 = f32[64,64,4,1,8]{1,4,3,2,0:T(8,128)S(1)} all-gather(f32[1,64,4,1,8]{1,4,3,2,0:T(8,128)S(1)} %bitcast.588), channel_id=1, replica_groups=mesh['seq'=64,'tp'=8] {'seq'}, dimensions={0}, use_global_device_ids=true | all-gather | bytes 532480 | tf_op jit(solution)/shard_map/all_gather | solution.py:14
  293.5 110.7 %all_gather.30 = f32[64,64,4,1,8]{1,4,3,2,0:T(8,128)} all-gather(f32[1,64,4,1,8]{1,4,3,2,0:T(8,128)S(1)} %bitcast.584), channel_id=1, replica_groups=mesh['seq'=64,'tp'=8] {'seq'}, dimensions={0}, use_global_device_ids=true | all-gather | bytes 532480 | tf_op jit(solution)/shard_map/all_gather | solution.py:14
  404.9 301.5 %all-gather.2.cloned.1.call-done = f32[64,64,4,1,8,128]{5,4,3,2,1,0:T(8,128)} async-done(((f32[1,64,4,1,8,128]{5,4,3,2,1,0:T(8,128)}), f32[64,64,4,1,8,128]{5,4,3,2,1,0:T(8,128)}) %all-gather.2.cloned.1.call-update) | async-done | bytes 67108880 | tf_op jit(solution)/shard_map/all_gather | solution.py:14
  707.8 184.2 %while.19 = (s32[]{:T(128)}, f32[64,4,1,8]{0,3,2,1:T(8,128)S(1)}, f32[64,4,1,8]{0,3,2,1:T(8,128)S(1)}, f32[64,4,1,8,128]{4,3,2,1,0:T(8,128)S(1)}, f32[64,64,4,1,...) while((s32[]{:T(128)}, f32[64,4,1,8]{0,3,2,1:T(8,128)S(1)}, ...), condition=%wide.region_25.26_spmd, body=%wide.region_24.25_spmd.sunk | while | flops 800773 | bytes 3301531 | solution.py:19
  708.8 1.9 fusion.182
  711.7 1.9 fusion.182
  714.7 1.9 fusion.182
  717.6 1.9 fusion.182
  720.5 1.9 fusion.182
  723.4 1.9 fusion.182
  726.3 1.9 fusion.182
  729.3 1.9 fusion.182
  732.2 1.9 fusion.182
  735.1 1.9 fusion.182
  738.0 1.9 fusion.182
  741.0 1.9 fusion.182
  743.9 1.9 fusion.182
  746.8 1.9 fusion.182
  749.7 1.9 fusion.182
  752.7 1.9 fusion.182
  755.6 1.9 fusion.182
  758.5 1.9 fusion.182
  761.4 1.9 fusion.182
  764.3 1.9 fusion.182
  767.3 1.9 fusion.182
  770.2 1.9 fusion.182
  773.1 1.9 fusion.182
  776.0 1.9 fusion.182
  779.0 1.9 fusion.182
  781.9 1.9 fusion.182
  784.8 1.9 fusion.182
  787.7 1.9 fusion.182
  790.6 1.9 fusion.182
  793.6 1.9 fusion.182
  796.5 1.9 fusion.182
  799.4 1.9 fusion.182
  802.3 1.9 fusion.182
  805.3 1.9 fusion.182
  808.2 1.9 fusion.182
  811.1 1.9 fusion.182
  814.0 1.9 fusion.182
  817.0 1.9 fusion.182
  819.9 1.9 fusion.182
  822.8 1.9 fusion.182
  825.7 1.9 fusion.182
  831.6 1.9 fusion.182
  837.4 1.9 fusion.182
  852.0 1.9 fusion.182
  872.5 1.9 fusion.182
  887.1 1.9 fusion.182
  893.6 36.2 %reduce-scatter.2.cloned.1.call-done = bf16[32,128]{1,0:T(8,128)(2,1)} async-done(((bf16[256,128]{1,0:T(8,128)(2,1)}), bf16[32,128]{1,0:T(8,128)(2,1)}) %reduce-scatter.2.cloned.1.call-update) | async-done | bytes 8208 | tf_op jit(solution)/shard_map/reduce_scatter | solution.py:170
  (599 shorter events, 147.0 us)
Async XLA Ops:
  6.5 162.1 %copy-start = (bf16[16,64,128]{2,1,0:T(8,128)(2,1)S(1)}, bf16[16,64,128]{2,1,0:T(8,128)(2,1)}, u32[]{:S(2)}) copy-start(bf16[16,64,128]{2,1,0:T(8,128)(2,1)} %param.22) | copy-start | bytes 786436
  6.5 699.9 %all-gather.2.cloned.1.call-start = ((), (), s32[]{:S(2)}) async-start(), calls=%async_computation.1 | async-start | bytes 68157440 | tf_op jit(solution)/shard_map/all_gather | solution.py:14
  119.1 7.0 copy-start.20
  122.5 3.5 copy-start.47
  122.5 5.5 copy-start.50
  122.5 6.7 copy-start.54
  122.6 10.8 %copy-start.61 = (pred[64]{0:T(512)(128)(4,1)}, pred[64]{0:T(512)(128)(4,1)S(1)}, u32[]{:S(2)}) copy-start(pred[64]{0:T(512)(128)(4,1)S(1)} %get-tuple-element.261) | copy-start | bytes 196
  122.6 13.3 %copy-start.65 = (pred[64]{0:T(512)(128)(4,1)}, pred[64]{0:T(512)(128)(4,1)S(1)}, u32[]{:S(2)}) copy-start(pred[64]{0:T(512)(128)(4,1)S(1)} %get-tuple-element.262) | copy-start | bytes 196
  122.6 14.6 %copy-start.69 = (pred[64]{0:T(512)(128)(4,1)}, pred[64]{0:T(512)(128)(4,1)S(1)}, u32[]{:S(2)}) copy-start(pred[64]{0:T(512)(128)(4,1)S(1)} %get-tuple-element.263) | copy-start | bytes 196
  122.6 17.2 %copy-start.73 = (pred[64]{0:T(512)(128)(4,1)}, pred[64]{0:T(512)(128)(4,1)S(1)}, u32[]{:S(2)}) copy-start(pred[64]{0:T(512)(128)(4,1)S(1)} %get-tuple-element.264) | copy-start | bytes 196
  122.6 18.7 %copy-start.77 = (pred[64]{0:T(512)(128)(4,1)}, pred[64]{0:T(512)(128)(4,1)S(1)}, u32[]{:S(2)}) copy-start(pred[64]{0:T(512)(128)(4,1)S(1)} %get-tuple-element.257) | copy-start | bytes 196
  126.1 3.1 copy-start.25
  128.1 17.9 %copy-start.14 = (f32[64,4,8]{0,2,1:T(8,128)}, f32[64,4,8]{0,2,1:T(8,128)S(1)}, u32[]{:S(2)}) copy-start(f32[64,4,8]{0,2,1:T(8,128)S(1)} %get-tuple-element.277) | copy-start | bytes 24580
  129.3 4.0 copy-start.27
  131.2 14.7 %copy-start.17 = (f32[64,4,8]{0,2,1:T(8,128)}, f32[64,4,8]{0,2,1:T(8,128)S(1)}, u32[]{:S(2)}) copy-start(f32[64,4,8]{0,2,1:T(8,128)S(1)} %get-tuple-element.279) | copy-start | bytes 24580
  131.3 4.5 copy-start.29
  139.9 2.5 copy-start.46
  139.9 4.0 copy-start.88
  139.9 4.0 copy-start.89
  139.9 4.0 copy-start.22
  139.9 4.0 copy-start.87
  140.6 3.8 copy-start.59
  140.6 4.7 copy-start.48
  140.6 4.7 copy-start.51
  140.6 4.7 copy-start.55
  140.6 5.3 copy-start.62
  140.6 5.3 copy-start.66
  140.6 5.3 copy-start.70
  140.7 5.3 copy-start.74
  141.4 4.6 copy-start.78
  142.5 7.0 copy-start.60
  143.9 4.2 copy-start.58
  144.3 3.7 copy-start.13
  165.9 9.4 %copy-start.4 = (bf16[64,4,8,192]{3,0,2,1:T(8,128)(2,1)S(1)}, bf16[64,4,8,192]{3,0,2,1:T(8,128)(2,1)}, u32[]{:S(2)}) copy-start(bf16[64,4,8,192]{3,0,2,1:T(8,128)(2,1)} %get-tuple-element.251) | copy-start | bytes 2359300
  169.9 7.1 copy-start.10
  169.9 7.1 copy-start.52
  184.8 3.9 copy-start.85
  184.8 3.9 copy-start.91
  184.8 5.2 copy-start.83
  184.8 5.2 copy-start.81
  184.9 5.3 copy-start.34
  184.9 5.4 copy-start.31
  184.9 5.4 copy-start.32
  184.9 5.4 copy-start.37
  184.9 5.4 copy-start.38
  184.9 5.4 copy-start.39
  184.9 5.4 copy-start.40
  184.9 5.4 copy-start.41
  184.9 5.4 copy-start.42
  184.9 5.4 copy-start.43
  185.0 5.4 copy-start.44
  185.0 5.4 copy-start.49
  185.0 5.4 copy-start.53
  185.0 5.4 copy-start.57
  185.0 5.4 copy-start.64
  185.0 5.4 copy-start.68
  185.0 5.4 copy-start.72
  185.0 5.4 copy-start.76
  185.0 5.4 copy-start.80
  185.0 5.4 copy-start.84
  185.1 5.7 copy-start.16
  185.1 5.7 copy-start.19
  189.9 739.8 %reduce-scatter.2.cloned.1.call-start = ((), (), s32[]{:S(2)}) async-start(), calls=%async_computation.2 | async-start | bytes 73728 | tf_op jit(solution)/shard_map/reduce_scatter | solution.py:170
  707.7 184.9 %copy-start.90 = (bf16[1024,128]{1,0:T(8,128)(2,1)S(1)}, bf16[1024,128]{1,0:T(8,128)(2,1)}, u32[]{:S(2)}) copy-start(bf16[1024,128]{1,0:T(8,128)(2,1)} %param.23) | copy-start | bytes 786436
  (30 other events, 49.2 us)
Sparse Core Ops, SparseCore 0:
  190.1 516.3 all-gather.1
  893.7 36.0 reduce-scatter.1
where the time goes:
time: 943 us; the launch traced here: 937 us
  waiting for transfers between devices  338 us (36%)
  blocking collectives  319 us (34%)
  other arithmetic  209 us (22%)
  local copies, waits for them, and re-layouts  29.6 us (3%)
  matrix products  23.3 us (2%)
  between operations  14.7 us (2%)
    all_gather x1, waiting for transfers between devices, merged(): gathered = jax.tree.map(lambda a: lax.all_gather(a, axis), part)  302 us
    all_gather x2, blocking collectives, merged(): gathered = jax.tree.map(lambda a: lax.all_gather(a, axis), part)  213 us
    add x63, other arithmetic, combine(): out_a * factor_a[..., None] + out_b * factor_b[..., None]  119 us
    all_gather x1, blocking collectives, local(): gathered = lax.all_gather(queries, 'seq', axis=0, tiled=True)  106 us
    mul x63, other arithmetic, combine(): out_b * factor_b[..., None]  46.8 us
    reduce_scatter x1, waiting for transfers between devices, local(): lax.psum_scatter(terms.astype(jnp.bfloat16), 'tp', scatter_dimension=0, t...  36.2 us
  transfers between devices with their start and end apart: 2, of which 2 were waited for; matrix products, arithmetic and copies ran while one was open for 0% of the time, Pallas kernels for 0%

commit v1 on v0

--- a/solution.py
+++ b/solution.py
@@ -64,7 +64,9 @@
     heads_local = kv_local * HPK
     score_scale = HEAD_DIM ** (-0.5)
     seq_idx = lax.axis_index("seq")
-    gathered = lax.all_gather(queries, "seq", axis=0, tiled=True)
+    gathered = jnp.concatenate(
+        lax.all_to_all(jnp.stack([queries] * lax.axis_size("seq")), "seq", 0, 0), axis=0
+    )
     query_all = gathered.reshape(requests, NEW, kv_local, HPK, HEAD_DIM)
     group_hot = group_of[:, None] == jnp.arange(GROUPS, dtype=jnp.int32)[None, :]
     own_prefix = jnp.sum(jnp.where(group_hot, prefix_len[None, :], 0), axis=1)

time: 943 us -> 857 us (0.909)
  blocking collectives: 319 us -> 214 us
  starting transfers between devices: 0.04 us -> 18.7 us
    all_gather x1 -> x0, blocking collectives: 106 us -> none  [local(): gathered = lax.all_gather(queries, 'seq', axis=0, tiled=True)]
    all_to_all x0 -> x1, starting transfers between devices: none -> 18.6 us  [local(): lax.all_to_all(jnp.stack([queries] * lax.axis_size('seq')), 'seq', 0, 0)]
    all_to_all x0 -> x1, waiting for transfers between devices: none -> 11.5 us  [local(): lax.all_to_all(jnp.stack([queries] * lax.axis_size('seq')), 'seq', 0, 0)]
  transfers between devices with their start and end apart: 2 -> 3, of which waited for: 2 -> 3; matrix products, arithmetic and copies ran while one was open for 0% -> 3% of each run, Pallas kernels for 0% -> 0%
where the time goes in v1:
time: 857 us; the launch traced here: 850 us
  waiting for transfers between devices  347 us (40%)
  blocking collectives  214 us (25%)
  other arithmetic  204 us (24%)
  local copies, waits for them, and re-layouts  30.6 us (4%)
  starting transfers between devices  18.7 us (2%)
  matrix products  17.8 us (2%)
  between operations  14.3 us (2%)
    all_gather x1, waiting for transfers between devices, merged(): gathered = jax.tree.map(lambda a: lax.all_gather(a, axis), part)  299 us
    all_gather x2, blocking collectives, merged(): gathered = jax.tree.map(lambda a: lax.all_gather(a, axis), part)  214 us
    add x63, other arithmetic, combine(): out_a * factor_a[..., None] + out_b * factor_b[..., None]  119 us
    mul x63, other arithmetic, combine(): out_b * factor_b[..., None]  46.8 us
    reduce_scatter x1, waiting for transfers between devices, local(): lax.psum_scatter(terms.astype(jnp.bfloat16), 'tp', scatter_dimension=0, t...  36.1 us
    all_to_all x1, starting transfers between devices, local(): lax.all_to_all(jnp.stack([queries] * lax.axis_size('seq')), 'seq', 0, 0)  18.6 us
  transfers between devices with their start and end apart: 3, of which 3 were waited for; matrix products, arithmetic and copies ran while one was open for 3% of the time, Pallas kernels for 0%

profile of v1, /device:TPU:2, one launch (start us, length us, event | category | flops | bytes accessed | tf_op | source)
XLA Modules:
  0.0 849.6 jit_solution(7345891739126153928)
XLA Ops:
  8.2 18.6 %all-to-all-start = ((bf16[64,1,4,1024]{3,2,1,0:T(4,128)(2,1)}), bf16[64,1,4,1024]{3,2,1,0:T(4,128)(2,1)S(1)}, u32[]{:S(2)}, u32[]{:S(2)}) async-start(bf16[64,1,4,1024]{3,2,1,0:T(4,128)(2,1)} %stack.2), calls=%async_computation | async-start | bytes 1048576 | tf_op jit(solution)/shard_map/all_to_all | solution.py:68
  47.0 11.5 %all-to-all-done = bf16[64,1,4,1024]{3,2,1,0:T(4,128)(2,1)S(1)} async-done(((bf16[64,1,4,1024]{3,2,1,0:T(4,128)(2,1)}), bf16[64,1,4,1024]{3,2,1,0:T(4,128)(2,1)S(1)}, u32[]{:S(2)}, u32[]{:S(2)}) %all-to-all-start) | async-done | bytes 524320 | tf_op jit(solution)/shard_map/all_to_all | solution.py:68
  67.7 2.3 fusion.59
  72.9 2.3 fusion.56
  75.3 2.3 fusion.55
  77.6 2.3 fusion.54
  79.9 2.5 fusion.53
  99.8 3.3 fusion.150
  105.7 103.1 %all_gather.23 = f32[64,64,4,1,8]{1,4,3,2,0:T(8,128)S(1)} all-gather(f32[1,64,4,1,8]{1,4,3,2,0:T(8,128)S(1)} %bitcast.589), channel_id=1, replica_groups=mesh['seq'=64,'tp'=8] {'seq'}, dimensions={0}, use_global_device_ids=true | all-gather | bytes 532480 | tf_op jit(solution)/shard_map/all_gather | solution.py:14
  208.7 110.8 %all_gather.26 = f32[64,64,4,1,8]{1,4,3,2,0:T(8,128)} all-gather(f32[1,64,4,1,8]{1,4,3,2,0:T(8,128)S(1)} %bitcast.585), channel_id=1, replica_groups=mesh['seq'=64,'tp'=8] {'seq'}, dimensions={0}, use_global_device_ids=true | all-gather | bytes 532480 | tf_op jit(solution)/shard_map/all_gather | solution.py:14
  320.3 299.2 %all-gather.2.cloned.1.call-done = f32[64,64,4,1,8,128]{5,4,3,2,1,0:T(8,128)} async-done(((f32[1,64,4,1,8,128]{5,4,3,2,1,0:T(8,128)}), f32[64,64,4,1,8,128]{5,4,3,2,1,0:T(8,128)}) %all-gather.2.cloned.1.call-update) | async-done | bytes 67108880 | tf_op jit(solution)/shard_map/all_gather | solution.py:14
  620.8 184.2 %while.19 = (s32[]{:T(128)}, f32[64,4,1,8]{0,3,2,1:T(8,128)S(1)}, f32[64,4,1,8]{0,3,2,1:T(8,128)S(1)}, f32[64,4,1,8,128]{4,3,2,1,0:T(8,128)S(1)}, f32[64,64,4,1,...) while((s32[]{:T(128)}, f32[64,4,1,8]{0,3,2,1:T(8,128)S(1)}, ...), condition=%wide.region_25.26_spmd, body=%wide.region_24.25_spmd.sunk | while | flops 800773 | bytes 3301531 | solution.py:19
  621.8 1.9 fusion.182
  624.7 1.9 fusion.182
  627.7 1.9 fusion.182
  630.6 1.9 fusion.182
  633.5 1.9 fusion.182
  636.4 1.9 fusion.182
  639.4 1.9 fusion.182
  642.3 1.9 fusion.182
  645.2 1.9 fusion.182
  648.1 1.9 fusion.182
  651.1 1.9 fusion.182
  654.0 1.9 fusion.182
  656.9 1.9 fusion.182
  659.8 1.9 fusion.182
  662.7 1.9 fusion.182
  665.7 1.9 fusion.182
  668.6 1.9 fusion.182
  671.5 1.9 fusion.182
  674.4 1.9 fusion.182
  677.4 1.9 fusion.182
  680.3 1.9 fusion.182
  683.2 1.9 fusion.182
  686.1 1.9 fusion.182
  689.0 1.9 fusion.182
  692.0 1.9 fusion.182
  694.9 1.9 fusion.182
  697.8 1.9 fusion.182
  700.7 1.9 fusion.182
  703.7 1.9 fusion.182
  706.6 1.9 fusion.182
  709.5 1.9 fusion.182
  712.4 1.9 fusion.182
  715.3 1.9 fusion.182
  718.3 1.9 fusion.182
  721.2 1.9 fusion.182
  724.1 1.9 fusion.182
  727.0 1.9 fusion.182
  730.0 1.9 fusion.182
  732.9 1.9 fusion.182
  735.8 1.9 fusion.182
  738.7 1.9 fusion.182
  741.7 1.9 fusion.182
  744.6 1.9 fusion.182
  747.5 1.9 fusion.182
  750.4 1.9 fusion.182
  753.3 1.9 fusion.182
  756.3 1.9 fusion.182
  759.2 1.9 fusion.182
  762.1 1.9 fusion.182
  773.8 1.9 fusion.182
  794.3 1.9 fusion.182
  806.6 36.1 %reduce-scatter.2.cloned.1.call-done = bf16[32,128]{1,0:T(8,128)(2,1)} async-done(((bf16[256,128]{1,0:T(8,128)(2,1)}), bf16[32,128]{1,0:T(8,128)(2,1)}) %reduce-scatter.2.cloned.1.call-update) | async-done | bytes 8208 | tf_op jit(solution)/shard_map/reduce_scatter | solution.py:172
  (525 shorter events, 140.9 us)
Async XLA Ops:
  6.5 78.0 %copy-start = (bf16[16,64,128]{2,1,0:T(8,128)(2,1)S(1)}, bf16[16,64,128]{2,1,0:T(8,128)(2,1)}, u32[]{:S(2)}) copy-start(bf16[16,64,128]{2,1,0:T(8,128)(2,1)} %param.22) | copy-start | bytes 786436
  6.5 52.8 %copy-start.8 = (bf16[8,192,128]{2,1,0:T(8,128)(2,1)S(1)}, bf16[8,192,128]{2,1,0:T(8,128)(2,1)}, u32[]{:S(2)}) copy-start(bf16[8,192,128]{2,1,0:T(8,128)(2,1)} %param.19) | copy-start | bytes 1179652
  8.2 50.3 %all-to-all-start = ((bf16[64,1,4,1024]{3,2,1,0:T(4,128)(2,1)}), bf16[64,1,4,1024]{3,2,1,0:T(4,128)(2,1)S(1)}, u32[]{:S(2)}, u32[]{:S(2)}) async-start(bf16[64,1,4,1024]{3,2,1,0:T(4,128)(2,1)} %stack.2), calls=%async_computation | async-start | bytes 1048576 | tf_op jit(solution)/shard_map/all_to_all | solution.py:68
  26.9 592.6 %all-gather.2.cloned.1.call-start = ((), (), s32[]{:S(2)}) async-start(), calls=%async_computation.2 | async-start | bytes 68157440 | tf_op jit(solution)/shard_map/all_gather | solution.py:14
  34.2 31.9 %copy-start.28 = (pred[64]{0:T(512)(128)(4,1)}, pred[64]{0:T(512)(128)(4,1)S(1)}, u32[]{:S(2)}) copy-start(pred[64]{0:T(512)(128)(4,1)S(1)} %get-tuple-element.258) | copy-start | bytes 196
  34.2 31.9 %copy-start.30 = (pred[64]{0:T(512)(128)(4,1)}, pred[64]{0:T(512)(128)(4,1)S(1)}, u32[]{:S(2)}) copy-start(pred[64]{0:T(512)(128)(4,1)S(1)} %get-tuple-element.259) | copy-start | bytes 196
  34.2 31.9 %copy-start.33 = (pred[64]{0:T(512)(128)(4,1)}, pred[64]{0:T(512)(128)(4,1)S(1)}, u32[]{:S(2)}) copy-start(pred[64]{0:T(512)(128)(4,1)S(1)} %get-tuple-element.260) | copy-start | bytes 196
  34.2 31.9 %copy-start.37 = (pred[64]{0:T(512)(128)(4,1)}, pred[64]{0:T(512)(128)(4,1)S(1)}, u32[]{:S(2)}) copy-start(pred[64]{0:T(512)(128)(4,1)S(1)} %get-tuple-element.261) | copy-start | bytes 196
  34.2 31.9 %copy-start.39 = (pred[64]{0:T(512)(128)(4,1)}, pred[64]{0:T(512)(128)(4,1)S(1)}, u32[]{:S(2)}) copy-start(pred[64]{0:T(512)(128)(4,1)S(1)} %get-tuple-element.262) | copy-start | bytes 196
  34.3 31.9 %copy-start.41 = (pred[64]{0:T(512)(128)(4,1)}, pred[64]{0:T(512)(128)(4,1)S(1)}, u32[]{:S(2)}) copy-start(pred[64]{0:T(512)(128)(4,1)S(1)} %get-tuple-element.263) | copy-start | bytes 196
  34.3 31.9 %copy-start.43 = (pred[64]{0:T(512)(128)(4,1)}, pred[64]{0:T(512)(128)(4,1)S(1)}, u32[]{:S(2)}) copy-start(pred[64]{0:T(512)(128)(4,1)S(1)} %get-tuple-element.264) | copy-start | bytes 196
  34.3 31.9 %copy-start.45 = (pred[64]{0:T(512)(128)(4,1)}, pred[64]{0:T(512)(128)(4,1)S(1)}, u32[]{:S(2)}) copy-start(pred[64]{0:T(512)(128)(4,1)S(1)} %get-tuple-element.257) | copy-start | bytes 196
  35.3 32.1 %copy-start.35 = (pred[16,64]{1,0:T(8,128)(4,1)}, pred[16,64]{1,0:T(8,128)(4,1)S(1)}, u32[]{:S(2)}) copy-start(pred[16,64]{1,0:T(8,128)(4,1)S(1)} %add_compare_fusion) | copy-start | bytes 3076
  46.9 12.5 %copy-start.11 = (pred[64,192]{1,0:T(8,128)(4,1)}, pred[64,192]{1,0:T(8,128)(4,1)S(1)}, u32[]{:S(2)}) copy-start(pred[64,192]{1,0:T(8,128)(4,1)S(1)} %broadcast_and_fusion) | copy-start | bytes 36868
  63.4 1.4 copy-start.10
  79.9 2.5 copy-start.12
  82.4 2.1 copy-start.36
  82.4 2.4 copy-start.49
  89.4 1.7 copy-start.4
  89.4 1.7 copy-start.9
  89.4 1.8 copy-start.31
  91.1 1.2 copy-start.3
  91.1 1.2 copy-start.34
  92.0 1.3 copy-start.2
  92.0 1.3 copy-start.38
  93.2 1.3 copy-start.1
  93.2 1.2 copy-start.40
  94.1 1.1 copy-start.42
  95.2 0.9 copy-start.44
  96.1 1.2 copy-start.6
  96.1 1.5 copy-start.7
  96.1 1.5 copy-start.17
  96.1 1.5 copy-start.18
  96.1 1.5 copy-start.46
  99.0 0.7 copy-start.15
  99.0 0.7 copy-start.27
  99.1 4.0 copy-start.51
  99.1 4.0 copy-start.53
  99.1 5.2 copy-start.48
  99.1 5.2 copy-start.47
  99.1 5.4 copy-start.16
  99.1 5.5 copy-start.13
  99.1 5.5 copy-start.14
  99.1 5.5 copy-start.19
  99.1 5.5 copy-start.20
  99.2 5.5 copy-start.21
  99.2 5.5 copy-start.22
  99.2 5.5 copy-start.23
  99.2 5.5 copy-start.24
  99.2 5.5 copy-start.25
  99.2 5.5 copy-start.26
  99.2 5.5 copy-start.29
  99.2 5.5 copy-start.32
  99.2 5.5 copy-start.50
  103.2 1.0 copy-start.5
  104.3 738.5 %reduce-scatter.2.cloned.1.call-start = ((), (), s32[]{:S(2)}) async-start(), calls=%async_computation.3 | async-start | bytes 73728 | tf_op jit(solution)/shard_map/reduce_scatter | solution.py:172
  620.8 184.9 %copy-start.52 = (bf16[1024,128]{1,0:T(8,128)(2,1)S(1)}, bf16[1024,128]{1,0:T(8,128)(2,1)}, u32[]{:S(2)}) copy-start(bf16[1024,128]{1,0:T(8,128)(2,1)} %param.23) | copy-start | bytes 786436
Sparse Core Ops, SparseCore 0:
  104.4 515.0 all-gather.1
  806.7 35.9 reduce-scatter.1
